TPU v7x, 256 devices: a whole 4x4x8 slice. The times are simulated.
256 devices in a mesh: row: 16 (over x, z_lo), col: 16 (over y, z_hi, core).
Axes of the slice: x: 4, y: 4, z: 8 (z_hi: 2, z_lo: 4; z = z_hi * 4 + z_lo), core: 2. Of those that a mesh axis runs over, the one named last changes fastest.
Arguments:
- hidden: bfloat16 [2560, 8192], P('row', 'col'), may hold values from -6 to 6
- w_query: bfloat16 [8192, 8192], P('col', 'row'), may hold values from -0.0625 to 0.0625
- w_keyval: bfloat16 [8192, 2048], P('col', 'row'), may hold values from -0.15625 to 0.15625
- prefix_cache: bfloat16 [2, 16384, 2048], P(None, 'col', 'row'), may hold values from -60 to 60, as said below
- suffix_lengths: int32 [16], replicated, may hold values from 32 to 160, as said below
- group_ids: int32 [16], replicated, may hold values from 0 to 1, as said below
Outputs:
- attended: bfloat16 [2560, 8192], P('col', 'row')
Inputs may be any that keep to these rules, and one draw needn't show every extreme that they name: `suffix_lengths`: every suffix has 32 to 160 live tokens; some request has exactly 160 and some exactly 32. `group_ids`: exactly 8 requests read each prefix. `prefix_cache`: finite values.
All inputs are finite; a program needn't handle non-finite values.
Results may differ from a plain program's by a relative error of at most 0.011.
Values may be sent and summed in bfloat16 or wider, within the bound.
No kernel may reach another device: no remote copies, remote signals or barrier semaphores. Data moves between devices by JAX's collectives and lax.ppermute only.
A program may use at most 128 MiB of HBM per device.

v0:
```python
import jax
import jax.numpy as jnp
from jax import lax
from jax.sharding import PartitionSpec as P

HD = 128
PREFIX = 16384
SUF = 160


def partner(value, axis, stride):
    mask = 2**stride
    pairs = [(source, source ^ mask) for source in range(lax.axis_size(axis))]
    return lax.ppermute(value, axis, pairs)


def rotary_tables(positions):
    freqs = 500000.0 ** (-(jnp.arange(HD // 2, dtype=jnp.float32) * 2.0 / HD))
    angles = positions.astype(jnp.float32)[:, None] * freqs[None, :]
    return (jnp.cos(angles), jnp.sin(angles))


def rotate(values, cosine, sine):
    first = values[..., : HD // 2]
    second = values[..., HD // 2 :]
    cosine = cosine[:, None, :]
    sine = sine[:, None, :]
    return jnp.concatenate(
        [first * cosine - second * sine, second * cosine + first * sine], axis=-1
    )


def block_size(count):
    size = count
    for _ in range(24):
        if size > 2048 and size % 2 == 0:
            size = size // 2
    return size


def block_stats(req_query, keys, values, scale):
    scores = jnp.einsum("thd,kd->htk", req_query, keys, preferred_element_type=jnp.float32) * scale
    top = jnp.max(scores, axis=-1)
    weights = jnp.exp(scores - top[..., None])
    total = jnp.sum(weights, axis=-1)
    accum = jnp.einsum(
        "htk,kd->htd", weights.astype(jnp.bfloat16), values, preferred_element_type=jnp.float32
    )
    return (top, total, accum)


def combine(first, second):
    top = jnp.maximum(first[0], second[0])
    scale_one = jnp.exp(first[0] - top)
    scale_two = jnp.exp(second[0] - top)
    total = first[1] * scale_one + second[1] * scale_two
    accum = first[2] * scale_one[..., None] + second[2] * scale_two[..., None]
    return (top, total, accum)


def empty_state(heads_here):
    return (
        jnp.full((heads_here, SUF), -1e30, jnp.float32),
        jnp.zeros((heads_here, SUF), jnp.float32),
        jnp.zeros((heads_here, SUF, HD), jnp.float32),
    )


def attend_keys(req_query, keys, values, scale):
    count = keys.shape[0]
    size = block_size(count)
    key_blocks = keys.reshape(count // size, size, HD)
    value_blocks = values.reshape(count // size, size, HD)

    def advance(state, pieces):
        return (combine(state, block_stats(req_query, pieces[0], pieces[1], scale)), None)

    state, _ = lax.scan(advance, empty_state(req_query.shape[1]), (key_blocks, value_blocks))
    return state


def flat_perm(n_row, n_col, target):
    pairs = []
    for r in range(n_row):
        for c in range(n_col):
            dest = target(r, c)
            if dest is not None:
                pairs.append((r * n_col + c, dest[0] * n_col + dest[1]))
    return pairs


def combine_all(states):
    top = states[0][0]
    for state in states[1:]:
        top = jnp.maximum(top, state[0])
    total = 0.0
    accum = 0.0
    for state in states:
        factor = jnp.exp(state[0] - top)
        total = total + state[1] * factor
        accum = accum + state[2] * factor[..., None]
    return (top, total, accum)


def per_device(hidden, w_query, w_keyval, prefix_cache, suffix_lengths, group_ids):
    n_row = lax.axis_size("row")
    n_col = lax.axis_size("col")
    row_id = lax.axis_index("row")
    col_id = lax.axis_index("col")
    heads_here = w_query.shape[1] // HD
    segments = w_keyval.shape[1] // HD
    scale = 1.0 / HD**0.5
    gathered = lax.all_gather(hidden, "row", axis=0, tiled=True)
    weights_all = jnp.concatenate([w_query, w_keyval], axis=1)
    tok_block = gathered.shape[0] // n_col
    projected = lax.psum_scatter(
        jnp.dot(gathered, weights_all, preferred_element_type=jnp.float32),
        "col",
        scatter_dimension=0,
        tiled=True,
    )
    positions = PREFIX + jnp.arange(tok_block, dtype=jnp.int32) % SUF
    cosine, sine = rotary_tables(positions)
    query = projected[:, : heads_here * HD].reshape(tok_block, heads_here, HD)
    query = rotate(query, cosine, sine).astype(jnp.bfloat16)
    keyval = projected[:, heads_here * HD :].reshape(tok_block, segments, HD)
    segment_ids = row_id * segments + jnp.arange(segments, dtype=jnp.int32)
    is_key = segment_ids % 2 == 0
    keyval = jnp.where(is_key[None, :, None], rotate(keyval, cosine, sine), keyval).astype(
        jnp.bfloat16
    )
    odd = row_id % 2
    is_even = odd == 0
    other_keyval, other_cache = partner((keyval, prefix_cache), "row", 0)
    suffix_keys = jnp.where(is_even, keyval[:, 0], other_keyval[:, 0])
    suffix_values = jnp.where(is_even, other_keyval[:, 0], keyval[:, 0])
    cache_keys = jnp.where(is_even, prefix_cache, other_cache)
    cache_values = jnp.where(is_even, other_cache, prefix_cache)
    kv_block = jnp.concatenate([cache_keys, cache_values], axis=-1)
    half_bit = 2
    handled = col_id ^ half_bit * odd
    masks = [m for m in range(1, n_col) if m & half_bit == 0]
    blocks = [lax.dynamic_index_in_dim(kv_block, group_ids[handled], 0, keepdims=False)]
    for mask in masks:
        peer_group = group_ids[col_id ^ mask ^ half_bit * odd]
        piece = lax.dynamic_index_in_dim(kv_block, peer_group, 0, keepdims=False)
        pairs = [(c, c ^ mask) for c in range(n_col)]
        blocks.append(lax.ppermute(piece, "col", pairs))
    half_kv = jnp.concatenate(blocks, axis=0)
    half_keys = half_kv[:, :HD]
    half_values = half_kv[:, HD:]
    axes = ("row", "col")
    cross = flat_perm(
        n_row, n_col, lambda r, c: (r ^ 1, c ^ half_bit) if r % 2 == 0 else (r ^ 1, c)
    )
    back = flat_perm(n_row, n_col, lambda r, c: (r ^ 1, c) if r % 2 == 0 else (r ^ 1, c ^ half_bit))
    same = flat_perm(n_row, n_col, lambda r, c: (r, c ^ half_bit) if r % 2 == 1 else None)
    q_cross = lax.ppermute(query, axes, cross)
    q_same = lax.ppermute(query, axes, same)
    q_first = jnp.where(is_even, query, q_cross)
    q_second = jnp.where(is_even, q_cross, q_same)
    q_all = jnp.concatenate([q_first, q_second], axis=1)
    half_state = attend_keys(q_all, half_keys, half_values, scale)
    mine = jax.tree.map(
        lambda a, b: jnp.where(is_even, a, b),
        jax.tree.map(lambda x: x[:heads_here], half_state),
        jax.tree.map(lambda x: x[heads_here:], half_state),
    )
    theirs = jax.tree.map(
        lambda a, b: jnp.where(is_even, a, b),
        jax.tree.map(lambda x: x[heads_here:], half_state),
        jax.tree.map(lambda x: x[:heads_here], half_state),
    )
    from_cross = lax.ppermute(theirs, axes, back)
    from_same = lax.ppermute(mine, axes, same)
    first_state = jax.tree.map(lambda a, b: jnp.where(is_even, a, b), mine, from_same)
    length = suffix_lengths[col_id]
    places = jnp.arange(SUF, dtype=jnp.int32)
    mask = (places[None, :] <= places[:, None]) & (places[None, :] < length)
    scores = (
        jnp.einsum("thd,kd->htk", query, suffix_keys, preferred_element_type=jnp.float32) * scale
    )
    scores = jnp.where(mask[None], scores, -1e30)
    own_top = jnp.max(scores, axis=-1)
    weights = jnp.exp(scores - own_top[..., None])
    own_total = jnp.sum(weights, axis=-1)
    own_accum = jnp.einsum(
        "htk,kd->htd",
        weights.astype(jnp.bfloat16),
        suffix_values,
        preferred_element_type=jnp.float32,
    )
    merged = combine_all([first_state, from_cross, (own_top, own_total, own_accum)])
    result = merged[2] / merged[1][..., None]
    live = (places < length).astype(jnp.float32)
    result = result * live[None, :, None]
    return jnp.transpose(result, (1, 0, 2)).reshape(tok_block, heads_here * HD).astype(jnp.bfloat16)


def solution(mesh):
    return jax.shard_map(
        per_device,
        mesh=mesh,
        in_specs=(
            P("row", "col"),
            P("col", "row"),
            P("col", "row"),
            P(None, "col", "row"),
            P(),
            P(),
        ),
        out_specs=P("col", "row"),
        check_vma=False,
    )
```

profile of v0, /device:TPU:32, one launch (start us, length us, event | category | flops | bytes accessed | tf_op | source)
XLA Modules:
  0.0 354.4 jit_solution(18435070876985730292)
XLA Ops:
  7.3 91.1 %all-gather.2.cloned.1.call-done = bf16[2560,512]{1,0:T(8,128)(2,1)} async-done(((bf16[160,512]{1,0:T(8,128)(2,1)}), bf16[2560,512]{1,0:T(8,128)(2,1)}) %all-gather.2.cloned.1.call-update) | async-done | bytes 2621456 | tf_op jit(solution)/shard_map/all_gather | solution.py:113
  98.4 6.6 %convolution_bitcast_fusion = f32[2560,640]{0,1:T(8,128)} fusion(bf16[2560,512]{1,0:T(8,128)(2,1)} %all-gather.2.cloned.1.call-done, bf16[512,128]{1,0:T(8,128)(2,1)} %param.10, bf16[512,512]{1,0:T(8,128)(2,1)} %param.9), kind=kOutput, calls=%fused_computation.22 | convolution fusion | flops 1679032320 | bytes 9830400 | tf_op jit(solution)/shard_map/dot_general | solution.py:117
  105.0 8.1 %copy.37 = f32[2560,640]{1,0:T(8,128)} copy(f32[2560,640]{0,1:T(8,128)} %convolution_bitcast_fusion) | data formatting | bytes 13107200
  139.3 3.7 %collective-permute-start.4 = (bf16[1024,256]{1,0:T(8,128)(2,1)S(1)}, bf16[1024,256]{1,0:T(8,128)(2,1)S(1)}, u32[]{:S(2)}, u32[]{:S(2)}) collective-permute-start(bf16[1024,256]{1,0:T(8,128)(2,1)S(1)} %get-tuple-element.101), channel_id=1, source_target_pairs={{0,8},{1,9},{2,10},{3,11},{4,12},{5,13},{6,14},{7,15},{8,0},{9,1},... | collective-permute-start | bytes 1572872 | tf_op jit(solution)/shard_map/ppermute | solution.py:148
  143.2 2.5 collective-permute-start.6
  149.7 11.7 %collective-permute-done.3 = bf16[1024,256]{1,0:T(8,128)(2,1)} collective-permute-done((bf16[1024,256]{1,0:T(8,128)(2,1)}, bf16[1024,256]{1,0:T(8,128)(2,1)}, u32[]{:S(2)}, u32[]{:S(2)}) %collective-permute-start.3) | collective-permute-done | bytes 524320 | tf_op jit(solution)/shard_map/ppermute | solution.py:148
  162.5 14.7 %collective-permute-done.4 = bf16[1024,256]{1,0:T(8,128)(2,1)S(1)} collective-permute-done((bf16[1024,256]{1,0:T(8,128)(2,1)S(1)}, bf16[1024,256]{1,0:T(8,128)(2,1)S(1)}, u32[]{:S(2)}, u32[]{:S(2)}) %collective-permute-start.4) | collective-permute-done | bytes 524320 | tf_op jit(solution)/shard_map/ppermute | solution.py:148
  177.2 11.4 %collective-permute-done.5 = bf16[1024,256]{1,0:T(8,128)(2,1)S(1)} collective-permute-done((bf16[1024,256]{1,0:T(8,128)(2,1)S(1)}, bf16[1024,256]{1,0:T(8,128)(2,1)S(1)}, u32[]{:S(2)}, u32[]{:S(2)}) %collective-permute-start.5) | collective-permute-done | bytes 524320 | tf_op jit(solution)/shard_map/ppermute | solution.py:148
  188.7 14.9 %collective-permute-done.7 = bf16[1024,256]{1,0:T(8,128)(2,1)S(1)} collective-permute-done((bf16[1024,256]{1,0:T(8,128)(2,1)S(1)}, bf16[1024,256]{1,0:T(8,128)(2,1)S(1)}, u32[]{:S(2)}, u32[]{:S(2)}) %collective-permute-start.7) | collective-permute-done | bytes 524320 | tf_op jit(solution)/shard_map/ppermute | solution.py:148
  205.2 32.0 %reduce-scatter.4.cloned.1.call-done = f32[160,640]{1,0:T(8,128)} async-done(((f32[2560,640]{1,0:T(8,128)}), f32[160,640]{1,0:T(8,128)}) %reduce-scatter.4.cloned.1.call-update) | async-done | bytes 409616
  245.7 2.5 collective-permute-start.13
  249.4 2.5 collective-permute-start.9
  252.4 2.0 fusion.70
  254.4 12.5 %collective-permute-done.8 = bf16[160,4,128]{2,0,1:T(8,128)(2,1)S(1)} collective-permute-done((bf16[160,4,128]{2,0,1:T(8,128)(2,1)S(1)}, bf16[160,4,128]{2,0,1:T(8,128)(2,1)S(1)}, u32[]{:S(2)}, u32[]{:S(2)}) %collective-permute-start.8) | collective-permute-done | bytes 163872 | tf_op jit(solution)/shard_map/ppermute | solution.py:158
  267.0 55.0 %while.15 = (s32[]{:T(128)}, f32[8,160]{1,0:T(8,128)S(1)}, f32[8,160]{1,0:T(8,128)S(1)}, f32[8,160,128]{2,1,0:T(8,128)S(1)}, bf16[4,2048,128]{2,1,0:T(8,128)(2,1...) while((s32[]{:T(128)}, f32[8,160]{1,0:T(8,128)S(1)}, ...), condition=%wide.region_4.5_spmd.clone, body=%wide.region_1.4_spmd.clone.sunk | while | flops 1363811840 | bytes 76168840 | solution.py:78
  267.0 2.7 bitcast_reduce_fusion.2
  269.7 4.0 %copy-done = f32[2048,160,8]{0,1,2:T(8,128)} copy-done((f32[2048,160,8]{0,1,2:T(8,128)}, f32[2048,160,8]{0,1,2:T(8,128)S(1)}, u32[]{:S(2)}) %copy-start) | copy-done | bytes 10485784 | tf_op jit(solution)/shard_map/while
  275.6 5.1 %fusion.85 = f32[8,160,128]{2,1,0:T(8,128)S(1)} fusion(f32[2048,160,8]{0,1,2:T(8,128)} %copy-done, f32[8,160]{1,0:T(8,128)S(1)} %get-tuple-element.181, f32[8,160,128]{2,1,0:T(8,128)S(1)} %get-tuple-element.198, bf16[4,2048,128]{2,1,0:T(8,128)(2,1)S(1)} %get-tuple-element.210, s32[]{:T(128)} %get-tuple-element.195, ...), kind=kOutput, calls=%fused_computation.7.clone.1 | convolution fusion | flops 679608320 | bytes 12345349 | tf_op jit(solution)/shard_map/while/body/eval_jaxpr/htk,kd->htd/dot_general | solution.py:46
  280.8 2.7 bitcast_reduce_fusion.2
  283.5 4.0 %copy-done = f32[2048,160,8]{0,1,2:T(8,128)} copy-done((f32[2048,160,8]{0,1,2:T(8,128)}, f32[2048,160,8]{0,1,2:T(8,128)S(1)}, u32[]{:S(2)}) %copy-start) | copy-done | bytes 10485784 | tf_op jit(solution)/shard_map/while
  289.4 5.1 %fusion.85 = f32[8,160,128]{2,1,0:T(8,128)S(1)} fusion(f32[2048,160,8]{0,1,2:T(8,128)} %copy-done, f32[8,160]{1,0:T(8,128)S(1)} %get-tuple-element.181, f32[8,160,128]{2,1,0:T(8,128)S(1)} %get-tuple-element.198, bf16[4,2048,128]{2,1,0:T(8,128)(2,1)S(1)} %get-tuple-element.210, s32[]{:T(128)} %get-tuple-element.195, ...), kind=kOutput, calls=%fused_computation.7.clone.1 | convolution fusion | flops 679608320 | bytes 12345349 | tf_op jit(solution)/shard_map/while/body/eval_jaxpr/htk,kd->htd/dot_general | solution.py:46
  294.6 2.7 bitcast_reduce_fusion.2
  297.2 4.0 %copy-done = f32[2048,160,8]{0,1,2:T(8,128)} copy-done((f32[2048,160,8]{0,1,2:T(8,128)}, f32[2048,160,8]{0,1,2:T(8,128)S(1)}, u32[]{:S(2)}) %copy-start) | copy-done | bytes 10485784 | tf_op jit(solution)/shard_map/while
  303.2 5.1 %fusion.85 = f32[8,160,128]{2,1,0:T(8,128)S(1)} fusion(f32[2048,160,8]{0,1,2:T(8,128)} %copy-done, f32[8,160]{1,0:T(8,128)S(1)} %get-tuple-element.181, f32[8,160,128]{2,1,0:T(8,128)S(1)} %get-tuple-element.198, bf16[4,2048,128]{2,1,0:T(8,128)(2,1)S(1)} %get-tuple-element.210, s32[]{:T(128)} %get-tuple-element.195, ...), kind=kOutput, calls=%fused_computation.7.clone.1 | convolution fusion | flops 679608320 | bytes 12345349 | tf_op jit(solution)/shard_map/while/body/eval_jaxpr/htk,kd->htd/dot_general | solution.py:46
  308.3 2.7 bitcast_reduce_fusion.2
  311.0 4.0 %copy-done = f32[2048,160,8]{0,1,2:T(8,128)} copy-done((f32[2048,160,8]{0,1,2:T(8,128)}, f32[2048,160,8]{0,1,2:T(8,128)S(1)}, u32[]{:S(2)}) %copy-start) | copy-done | bytes 10485784 | tf_op jit(solution)/shard_map/while
  316.9 5.1 %fusion.85 = f32[8,160,128]{2,1,0:T(8,128)S(1)} fusion(f32[2048,160,8]{0,1,2:T(8,128)} %copy-done, f32[8,160]{1,0:T(8,128)S(1)} %get-tuple-element.181, f32[8,160,128]{2,1,0:T(8,128)S(1)} %get-tuple-element.198, bf16[4,2048,128]{2,1,0:T(8,128)(2,1)S(1)} %get-tuple-element.210, s32[]{:T(128)} %get-tuple-element.195, ...), kind=kOutput, calls=%fused_computation.7.clone.1 | convolution fusion | flops 679608320 | bytes 12345349 | tf_op jit(solution)/shard_map/while/body/eval_jaxpr/htk,kd->htd/dot_general | solution.py:46
  322.1 3.8 %collective-permute-start.10 = (f32[4,160,128]{2,1,0:T(8,128)S(1)}, f32[4,160,128]{2,1,0:T(8,128)S(1)}, u32[]{:S(2)}, u32[]{:S(2)}) collective-permute-start(f32[4,160,128]{2,1,0:T(8,128)S(1)} %get-tuple-element.107), channel_id=1, source_target_pairs={{16,18},{17,19},{18,16},{19,17},{20,22},{21,23},{22,20},{23,21},{2... | collective-permute-start | bytes 983048 | tf_op jit(solution)/shard_map/ppermute | solution.py:175
  326.0 6.0 %collective-permute-start.11 = (f32[4,160]{1,0:T(4,128)S(1)}, f32[4,160]{1,0:T(4,128)S(1)}, u32[]{:S(2)}, u32[]{:S(2)}) collective-permute-start(f32[4,160]{1,0:T(4,128)S(1)} %get-tuple-element.115), channel_id=1, source_target_pairs={{16,18},{17,19},{18,16},{19,17},{20,22},{21,23},{22,20},{23,21},{2... | collective-permute-start | bytes 7688 | tf_op jit(solution)/shard_map/ppermute | solution.py:175
  332.1 3.8 %collective-permute-start.15 = (f32[4,160]{1,0:T(4,128)S(1)}, f32[4,160]{1,0:T(4,128)S(1)}, u32[]{:S(2)}, u32[]{:S(2)}) collective-permute-start(f32[4,160]{1,0:T(4,128)S(1)} %get-tuple-element.117), channel_id=1, source_target_pairs={{16,18},{17,19},{18,16},{19,17},{20,22},{21,23},{22,20},{23,21},{2... | collective-permute-start | bytes 7688 | tf_op jit(solution)/shard_map/ppermute | solution.py:175
  335.9 5.6 %collective-permute-done.11 = f32[4,160]{1,0:T(4,128)S(1)} collective-permute-done((f32[4,160]{1,0:T(4,128)S(1)}, f32[4,160]{1,0:T(4,128)S(1)}, u32[]{:S(2)}, u32[]{:S(2)}) %collective-permute-start.11) | collective-permute-done | bytes 2592 | tf_op jit(solution)/shard_map/ppermute | solution.py:175
  342.7 2.4 collective-permute-done.16
  (95 shorter events, 39.9 us)
Async XLA Ops:
  6.5 91.9 %all-gather.2.cloned.1.call-start = ((), (), s32[]{:S(2)}) async-start(), calls=%async_computation.1 | async-start | bytes 2785280 | tf_op jit(solution)/shard_map/all_gather | solution.py:113
  7.3 230.0 %reduce-scatter.4.cloned.1.call-start = ((), (), s32[]{:S(2)}) async-start(), calls=%async_computation.2 | async-start | bytes 6963200
  113.2 1.0 copy-start.1
  113.2 2.2 copy-start.4
  113.2 14.9 %copy-start.7 = (s32[16]{0:T(128)S(1)}, s32[16]{0:T(128)}, u32[]{:S(2)}) copy-start(s32[16]{0:T(128)} %param.12) | copy-start | bytes 196
  114.2 16.2 %collective-permute-start = (bf16[2,1024,128]{2,1,0:T(8,128)(2,1)S(1)}, bf16[2,1024,128]{2,1,0:T(8,128)(2,1)S(1)}, u32[]{:S(2)}, u32[]{:S(2)}) collective-permute-start(bf16[2,1024,128]{2,1,0:T(8,128)(2,1)S(1)} %copy-done.1), channel_id=1, source_target_pairs={{0,16},{16,0},{32,48},{48,32},{64,80},{80,64},{96,112},{112,96},{1... | collective-permute-start | bytes 1572872 | tf_op jit(solution)/shard_map/ppermute | solution.py:14
  128.7 8.8 %copy-start.6 = (f32[64]{0:T(128)}, f32[64]{0:T(128)S(1)}, u32[]{:S(2)}) copy-start(f32[64]{0:T(128)S(1)} %negate_power_fusion) | copy-start | bytes 772
  129.4 8.1 %copy-start.5 = (f32[160]{0:T(256)}, f32[160]{0:T(256)S(1)}, u32[]{:S(2)}) copy-start(f32[160]{0:T(256)S(1)} %add_convert_fusion.1) | copy-start | bytes 1924
  131.9 11.4 %collective-permute-start.1 = (bf16[1024,256]{1,0:T(8,128)(2,1)}, bf16[1024,256]{1,0:T(8,128)(2,1)}, u32[]{:S(2)}, u32[]{:S(2)}) collective-permute-start(bf16[1024,256]{1,0:T(8,128)(2,1)} %get-tuple-element.98), channel_id=1, source_target_pairs={{0,1},{1,0},{2,3},{3,2},{4,5},{5,4},{6,7},{7,6},{8,9},{9,8},{10,11... | collective-permute-start | bytes 1572872 | tf_op jit(solution)/shard_map/ppermute | solution.py:148
  131.9 15.1 %collective-permute-start.2 = (bf16[1024,256]{1,0:T(8,128)(2,1)}, bf16[1024,256]{1,0:T(8,128)(2,1)}, u32[]{:S(2)}, u32[]{:S(2)}) collective-permute-start(bf16[1024,256]{1,0:T(8,128)(2,1)} %get-tuple-element.99), channel_id=1, source_target_pairs={{0,4},{1,5},{2,6},{3,7},{4,0},{5,1},{6,2},{7,3},{8,12},{9,13},{10,... | collective-permute-start | bytes 1572872 | tf_op jit(solution)/shard_map/ppermute | solution.py:148
  134.2 27.2 %collective-permute-start.3 = (bf16[1024,256]{1,0:T(8,128)(2,1)}, bf16[1024,256]{1,0:T(8,128)(2,1)}, u32[]{:S(2)}, u32[]{:S(2)}) collective-permute-start(bf16[1024,256]{1,0:T(8,128)(2,1)} %get-tuple-element.100), channel_id=1, source_target_pairs={{0,5},{1,4},{2,7},{3,6},{4,1},{5,0},{6,3},{7,2},{8,13},{9,12},{10,... | collective-permute-start | bytes 1572872 | tf_op jit(solution)/shard_map/ppermute | solution.py:148
  139.3 37.9 %collective-permute-start.4 = (bf16[1024,256]{1,0:T(8,128)(2,1)S(1)}, bf16[1024,256]{1,0:T(8,128)(2,1)S(1)}, u32[]{:S(2)}, u32[]{:S(2)}) collective-permute-start(bf16[1024,256]{1,0:T(8,128)(2,1)S(1)} %get-tuple-element.101), channel_id=1, source_target_pairs={{0,8},{1,9},{2,10},{3,11},{4,12},{5,13},{6,14},{7,15},{8,0},{9,1},... | collective-permute-start | bytes 1572872 | tf_op jit(solution)/shard_map/ppermute | solution.py:148
  143.1 45.5 %collective-permute-start.5 = (bf16[1024,256]{1,0:T(8,128)(2,1)S(1)}, bf16[1024,256]{1,0:T(8,128)(2,1)S(1)}, u32[]{:S(2)}, u32[]{:S(2)}) collective-permute-start(bf16[1024,256]{1,0:T(8,128)(2,1)S(1)} %get-tuple-element.102), channel_id=1, source_target_pairs={{0,9},{1,8},{2,11},{3,10},{4,13},{5,12},{6,15},{7,14},{8,1},{9,0},... | collective-permute-start | bytes 1572872 | tf_op jit(solution)/shard_map/ppermute | solution.py:148
  143.2 45.4 %collective-permute-start.6 = (bf16[1024,256]{1,0:T(8,128)(2,1)S(1)}, bf16[1024,256]{1,0:T(8,128)(2,1)S(1)}, u32[]{:S(2)}, u32[]{:S(2)}) collective-permute-start(bf16[1024,256]{1,0:T(8,128)(2,1)S(1)} %fusion.43), channel_id=1, source_target_pairs={{0,12},{1,13},{2,14},{3,15},{4,8},{5,9},{6,10},{7,11},{8,4},{9,5},... | collective-permute-start | bytes 1572872 | tf_op jit(solution)/shard_map/ppermute | solution.py:148
  147.0 56.6 %collective-permute-start.7 = (bf16[1024,256]{1,0:T(8,128)(2,1)S(1)}, bf16[1024,256]{1,0:T(8,128)(2,1)S(1)}, u32[]{:S(2)}, u32[]{:S(2)}) collective-permute-start(bf16[1024,256]{1,0:T(8,128)(2,1)S(1)} %get-tuple-element.97), channel_id=1, source_target_pairs={{0,13},{1,12},{2,15},{3,14},{4,9},{5,8},{6,11},{7,10},{8,5},{9,4},... | collective-permute-start | bytes 1572872 | tf_op jit(solution)/shard_map/ppermute | solution.py:148
  245.7 21.3 %copy-start.2 = (bf16[160,128]{0,1:T(8,128)(2,1)}, bf16[160,128]{0,1:T(8,128)(2,1)S(1)}, u32[]{:S(2)}) copy-start(bf16[160,128]{0,1:T(8,128)(2,1)S(1)} %fusion.52) | copy-start | bytes 122884
  245.7 6.7 %collective-permute-start.13 = (bf16[160,1,128]{0,2,1:T(8,128)(2,1)S(1)}, bf16[160,1,128]{0,2,1:T(8,128)(2,1)S(1)}, u32[]{:S(2)}, u32[]{:S(2)}) collective-permute-start(bf16[160,1,128]{0,2,1:T(8,128)(2,1)S(1)} %bitcast.113), channel_id=1, source_target_pairs={{0,16},{16,0},{32,48},{48,32},{64,80},{80,64},{96,112},{112,96},{1... | collective-permute-start | bytes 122888 | tf_op jit(solution)/shard_map/ppermute | solution.py:14
  249.3 17.6 %collective-permute-start.8 = (bf16[160,4,128]{2,0,1:T(8,128)(2,1)S(1)}, bf16[160,4,128]{2,0,1:T(8,128)(2,1)S(1)}, u32[]{:S(2)}, u32[]{:S(2)}) collective-permute-start(bf16[160,4,128]{2,0,1:T(8,128)(2,1)S(1)} %pad_maximum_fusion.1), channel_id=1, source_target_pairs={{0,18},{1,19},{2,16},{3,17},{4,22},{5,23},{6,20},{7,21},{8,26},{9,... | collective-permute-start | bytes 491528 | tf_op jit(solution)/shard_map/ppermute | solution.py:158
  249.4 17.5 %collective-permute-start.9 = (bf16[160,4,128]{2,0,1:T(8,128)(2,1)S(1)}, bf16[160,4,128]{2,0,1:T(8,128)(2,1)S(1)}, u32[]{:S(2)}, u32[]{:S(2)}) collective-permute-start(bf16[160,4,128]{2,0,1:T(8,128)(2,1)S(1)} %pad_maximum_fusion.1), channel_id=1, source_target_pairs={{16,18},{17,19},{18,16},{19,17},{20,22},{21,23},{22,20},{23,21},{2... | collective-permute-start | bytes 491528 | tf_op jit(solution)/shard_map/ppermute | solution.py:159
  267.0 78.2 %copy-start.3 = (bf16[160,128]{0,1:T(8,128)(2,1)S(1)}, bf16[160,128]{0,1:T(8,128)(2,1)}, u32[]{:S(2)}) copy-start(bf16[160,128]{0,1:T(8,128)(2,1)} %copy-done.2) | copy-start | bytes 122884
  267.0 78.2 %copy-start.8 = (f32[160]{0:T(256)S(1)}, f32[160]{0:T(256)}, u32[]{:S(2)}) copy-start(f32[160]{0:T(256)} %fusion.66) | copy-start | bytes 1924
  269.7 4.0 %copy-start = (f32[2048,160,8]{0,1,2:T(8,128)}, f32[2048,160,8]{0,1,2:T(8,128)S(1)}, u32[]{:S(2)}) copy-start(f32[2048,160,8]{0,1,2:T(8,128)S(1)} %get-tuple-element.180) | copy-start | bytes 31457284 | tf_op jit(solution)/shard_map/while
  283.5 4.0 %copy-start = (f32[2048,160,8]{0,1,2:T(8,128)}, f32[2048,160,8]{0,1,2:T(8,128)S(1)}, u32[]{:S(2)}) copy-start(f32[2048,160,8]{0,1,2:T(8,128)S(1)} %get-tuple-element.180) | copy-start | bytes 31457284 | tf_op jit(solution)/shard_map/while
  297.2 4.0 %copy-start = (f32[2048,160,8]{0,1,2:T(8,128)}, f32[2048,160,8]{0,1,2:T(8,128)S(1)}, u32[]{:S(2)}) copy-start(f32[2048,160,8]{0,1,2:T(8,128)S(1)} %get-tuple-element.180) | copy-start | bytes 31457284 | tf_op jit(solution)/shard_map/while
  311.0 4.0 %copy-start = (f32[2048,160,8]{0,1,2:T(8,128)}, f32[2048,160,8]{0,1,2:T(8,128)S(1)}, u32[]{:S(2)}) copy-start(f32[2048,160,8]{0,1,2:T(8,128)S(1)} %get-tuple-element.180) | copy-start | bytes 31457284 | tf_op jit(solution)/shard_map/while
  322.1 23.0 %collective-permute-start.10 = (f32[4,160,128]{2,1,0:T(8,128)S(1)}, f32[4,160,128]{2,1,0:T(8,128)S(1)}, u32[]{:S(2)}, u32[]{:S(2)}) collective-permute-start(f32[4,160,128]{2,1,0:T(8,128)S(1)} %get-tuple-element.107), channel_id=1, source_target_pairs={{16,18},{17,19},{18,16},{19,17},{20,22},{21,23},{22,20},{23,21},{2... | collective-permute-start | bytes 983048 | tf_op jit(solution)/shard_map/ppermute | solution.py:175
  325.9 19.2 %collective-permute-start.14 = (f32[4,160,128]{2,1,0:T(8,128)S(1)}, f32[4,160,128]{2,1,0:T(8,128)S(1)}, u32[]{:S(2)}, u32[]{:S(2)}) collective-permute-start(f32[4,160,128]{2,1,0:T(8,128)S(1)} %get-tuple-element.108), channel_id=1, source_target_pairs={{0,16},{1,17},{2,18},{3,19},{4,20},{5,21},{6,22},{7,23},{8,24},{9,... | collective-permute-start | bytes 983048 | tf_op jit(solution)/shard_map/ppermute | solution.py:174
  326.0 15.5 %collective-permute-start.11 = (f32[4,160]{1,0:T(4,128)S(1)}, f32[4,160]{1,0:T(4,128)S(1)}, u32[]{:S(2)}, u32[]{:S(2)}) collective-permute-start(f32[4,160]{1,0:T(4,128)S(1)} %get-tuple-element.115), channel_id=1, source_target_pairs={{16,18},{17,19},{18,16},{19,17},{20,22},{21,23},{22,20},{23,21},{2... | collective-permute-start | bytes 7688 | tf_op jit(solution)/shard_map/ppermute | solution.py:175
  332.0 10.7 %collective-permute-start.12 = (f32[4,160]{1,0:T(4,128)S(1)}, f32[4,160]{1,0:T(4,128)S(1)}, u32[]{:S(2)}, u32[]{:S(2)}) collective-permute-start(f32[4,160]{1,0:T(4,128)S(1)} %get-tuple-element.116), channel_id=1, source_target_pairs={{0,16},{1,17},{2,18},{3,19},{4,20},{5,21},{6,22},{7,23},{8,24},{9,... | collective-permute-start | bytes 7688 | tf_op jit(solution)/shard_map/ppermute | solution.py:174
  332.1 10.6 %collective-permute-start.15 = (f32[4,160]{1,0:T(4,128)S(1)}, f32[4,160]{1,0:T(4,128)S(1)}, u32[]{:S(2)}, u32[]{:S(2)}) collective-permute-start(f32[4,160]{1,0:T(4,128)S(1)} %get-tuple-element.117), channel_id=1, source_target_pairs={{16,18},{17,19},{18,16},{19,17},{20,22},{21,23},{22,20},{23,21},{2... | collective-permute-start | bytes 7688 | tf_op jit(solution)/shard_map/ppermute | solution.py:175
  341.5 3.6 %collective-permute-start.16 = (f32[4,160]{1,0:T(4,128)S(1)}, f32[4,160]{1,0:T(4,128)S(1)}, u32[]{:S(2)}, u32[]{:S(2)}) collective-permute-start(f32[4,160]{1,0:T(4,128)S(1)} %get-tuple-element.118), channel_id=1, source_target_pairs={{0,16},{1,17},{2,18},{3,19},{4,20},{5,21},{6,22},{7,23},{8,24},{9,... | collective-permute-start | bytes 7688 | tf_op jit(solution)/shard_map/ppermute | solution.py:174
Sparse Core Ops, SparseCore 0:
  9.1 89.2 all-gather.1
  113.3 123.8 reduce-scatter.3
where the time goes:
time: 356 us; the launch traced here: 354 us
  waiting for transfers between devices  198 us (56%)
  matrix products  41.5 us (12%)
  local copies, waits for them, and re-layouts  39.7 us (11%)
  starting transfers between devices  29.7 us (8%)
  between operations  29.4 us (8%)
  other arithmetic  16.2 us (5%)
    all_gather x1, waiting for transfers between devices, per_device(): gathered = lax.all_gather(hidden, 'row', axis=0, tiled=True)  91.1 us
    ppermute x7, waiting for transfers between devices, per_device(): blocks.append(lax.ppermute(piece, 'col', pairs))  52.8 us
    unnamed x3, waiting for transfers between devices  32.7 us
    dot_general x4, matrix products, block_stats(): jnp.einsum('htk,kd->htd', weights.astype(jnp.bfloat16), values, preferred...  20.6 us
    while x8, local copies, waits for them, and re-layouts  16.1 us
    unnamed x27, local copies, waits for them, and re-layouts  16 us
    ppermute x3, starting transfers between devices, per_device(): from_same = lax.ppermute(mine, axes, same)  13.5 us
    ppermute x1, waiting for transfers between devices, per_device(): q_cross = lax.ppermute(query, axes, cross)  12.5 us
  transfers between devices with their start and end apart: 19, of which 11 were waited for; matrix products, arithmetic and copies ran while one was open for 4% of the time, Pallas kernels for 0%

commit v1 on v0

--- a/solution.py
+++ b/solution.py
@@ -110,7 +110,9 @@
     heads_here = w_query.shape[1] // HD
     segments = w_keyval.shape[1] // HD
     scale = 1.0 / HD**0.5
-    gathered = lax.all_gather(hidden, "row", axis=0, tiled=True)
+    gathered = jnp.concatenate(
+        lax.all_to_all(jnp.stack([hidden] * lax.axis_size("row")), "row", 0, 0), axis=0
+    )
     weights_all = jnp.concatenate([w_query, w_keyval], axis=1)
     tok_block = gathered.shape[0] // n_col
     projected = lax.psum_scatter(

time: 356 us -> 331 us (0.930)
  waiting for transfers between devices: 198 us -> 106 us
  blocking collectives: 0 us -> 67.5 us
    all_gather x1 -> x0, waiting for transfers between devices: 91.1 us -> none  [per_device(): gathered = lax.all_gather(hidden, 'row', axis=0, tiled=True)]
    all_to_all x0 -> x1, blocking collectives: none -> 67.5 us  [per_device(): lax.all_to_all(jnp.stack([hidden] * lax.axis_size('row')), 'row', 0, 0)]
    unnamed x3 -> x2, waiting for transfers between devices: 32.7 us -> 31.6 us
    unnamed x27 -> x31, local copies, waits for them, and re-layouts: 16 us -> 16 us
  transfers between devices with their start and end apart: 19 -> 18, of which waited for: 11 -> 10; matrix products, arithmetic and copies ran while one was open for 4% -> 5% of each run, Pallas kernels for 0% -> 0%
where the time goes in v1:
time: 331 us; the launch traced here: 330 us
  waiting for transfers between devices  106 us (32%)
  blocking collectives  67.5 us (20%)
  local copies, waits for them, and re-layouts  40.8 us (12%)
  matrix products  39.5 us (12%)
  starting transfers between devices  31.1 us (9%)
  between operations  29 us (9%)
  other arithmetic  16.1 us (5%)
    all_to_all x1, blocking collectives, per_device(): lax.all_to_all(jnp.stack([hidden] * lax.axis_size('row')), 'row', 0, 0)  67.5 us
    ppermute x7, waiting for transfers between devices, per_device(): blocks.append(lax.ppermute(piece, 'col', pairs))  52.9 us
    unnamed x2, waiting for transfers between devices  31.6 us
    dot_general x4, matrix products, block_stats(): jnp.einsum('htk,kd->htd', weights.astype(jnp.bfloat16), values, preferred...  20.5 us
    while x8, local copies, waits for them, and re-layouts  16 us
    unnamed x31, local copies, waits for them, and re-layouts  16 us
    ppermute x3, starting transfers between devices, per_device(): from_same = lax.ppermute(mine, axes, same)  13.6 us
    ppermute x1, waiting for transfers between devices, per_device(): q_cross = lax.ppermute(query, axes, cross)  12.5 us
  transfers between devices with their start and end apart: 18, of which 10 were waited for; matrix products, arithmetic and copies ran while one was open for 5% of the time, Pallas kernels for 0%

profile of v1, /device:TPU:32, one launch (start us, length us, event | category | flops | bytes accessed | tf_op | source)
XLA Modules:
  0.0 330.0 jit_solution(7258325878981902189)
XLA Ops:
  7.8 67.5 %all_to_all.5 = bf16[16,160,512]{2,1,0:T(8,128)(2,1)S(1)} all-to-all(bf16[16,160,512]{2,1,0:T(8,128)(2,1)S(1)} %stack.2), channel_id=1, replica_groups=mesh['row'=16,'col'=16] {'row'}, dimensions={0} | all-to-all | bytes 5242880 | tf_op jit(solution)/shard_map/all_to_all | solution.py:114
  75.3 4.7 %convolution_bitcast_fusion = f32[2560,640]{0,1:T(8,128)} fusion(bf16[2560,512]{1,0:T(8,128)(2,1)S(1)} %bitcast.112, bf16[512,128]{1,0:T(8,128)(2,1)S(1)} %copy-done.8, bf16[512,512]{1,0:T(8,128)(2,1)S(1)} %copy-done.7), kind=kOutput, calls=%fused_computation.22 | convolution fusion | flops 1679032320 | bytes 9830400 | tf_op jit(solution)/shard_map/dot_general | solution.py:119
  80.0 8.1 %copy.37 = f32[2560,640]{1,0:T(8,128)} copy(f32[2560,640]{0,1:T(8,128)} %convolution_bitcast_fusion) | data formatting | bytes 13107200
  89.2 2.3 collective-permute-start
  114.9 3.3 collective-permute-start.4
  118.4 3.0 collective-permute-start.6
  125.6 11.6 %collective-permute-done.3 = bf16[1024,256]{1,0:T(8,128)(2,1)} collective-permute-done((bf16[1024,256]{1,0:T(8,128)(2,1)}, bf16[1024,256]{1,0:T(8,128)(2,1)}, u32[]{:S(2)}, u32[]{:S(2)}) %collective-permute-start.3) | collective-permute-done | bytes 524320 | tf_op jit(solution)/shard_map/ppermute | solution.py:150
  138.2 14.8 %collective-permute-done.4 = bf16[1024,256]{1,0:T(8,128)(2,1)S(1)} collective-permute-done((bf16[1024,256]{1,0:T(8,128)(2,1)S(1)}, bf16[1024,256]{1,0:T(8,128)(2,1)S(1)}, u32[]{:S(2)}, u32[]{:S(2)}) %collective-permute-start.4) | collective-permute-done | bytes 524320 | tf_op jit(solution)/shard_map/ppermute | solution.py:150
  153.0 11.4 %collective-permute-done.5 = bf16[1024,256]{1,0:T(8,128)(2,1)S(1)} collective-permute-done((bf16[1024,256]{1,0:T(8,128)(2,1)S(1)}, bf16[1024,256]{1,0:T(8,128)(2,1)S(1)}, u32[]{:S(2)}, u32[]{:S(2)}) %collective-permute-start.5) | collective-permute-done | bytes 524320 | tf_op jit(solution)/shard_map/ppermute | solution.py:150
  164.5 15.0 %collective-permute-done.7 = bf16[1024,256]{1,0:T(8,128)(2,1)S(1)} collective-permute-done((bf16[1024,256]{1,0:T(8,128)(2,1)S(1)}, bf16[1024,256]{1,0:T(8,128)(2,1)S(1)}, u32[]{:S(2)}, u32[]{:S(2)}) %collective-permute-start.7) | collective-permute-done | bytes 524320 | tf_op jit(solution)/shard_map/ppermute | solution.py:150
  181.2 31.6 %reduce-scatter.4.cloned.1.call-done = f32[160,640]{1,0:T(8,128)} async-done(((f32[2560,640]{1,0:T(8,128)}), f32[160,640]{1,0:T(8,128)}) %reduce-scatter.4.cloned.1.call-update) | async-done | bytes 409616
  221.3 2.5 collective-permute-start.13
  225.0 2.5 collective-permute-start.9
  229.9 12.5 %collective-permute-done.8 = bf16[160,4,128]{2,0,1:T(8,128)(2,1)S(1)} collective-permute-done((bf16[160,4,128]{2,0,1:T(8,128)(2,1)S(1)}, bf16[160,4,128]{2,0,1:T(8,128)(2,1)S(1)}, u32[]{:S(2)}, u32[]{:S(2)}) %collective-permute-start.8) | collective-permute-done | bytes 163872 | tf_op jit(solution)/shard_map/ppermute | solution.py:160
  242.6 55.0 %while.15 = (s32[]{:T(128)}, f32[8,160]{1,0:T(8,128)S(1)}, f32[8,160]{1,0:T(8,128)S(1)}, f32[8,160,128]{2,1,0:T(8,128)S(1)}, bf16[4,2048,128]{2,1,0:T(8,128)(2,1...) while((s32[]{:T(128)}, f32[8,160]{1,0:T(8,128)S(1)}, ...), condition=%wide.region_4.5_spmd.clone, body=%wide.region_1.4_spmd.clone.sunk | while | flops 1363811840 | bytes 76168840 | solution.py:78
  242.6 2.7 bitcast_reduce_fusion.2
  245.2 4.0 %copy-done = f32[2048,160,8]{0,1,2:T(8,128)} copy-done((f32[2048,160,8]{0,1,2:T(8,128)}, f32[2048,160,8]{0,1,2:T(8,128)S(1)}, u32[]{:S(2)}) %copy-start) | copy-done | bytes 10485784 | tf_op jit(solution)/shard_map/while
  251.1 5.1 %fusion.85 = f32[8,160,128]{2,1,0:T(8,128)S(1)} fusion(f32[2048,160,8]{0,1,2:T(8,128)} %copy-done, f32[8,160]{1,0:T(8,128)S(1)} %get-tuple-element.181, f32[8,160,128]{2,1,0:T(8,128)S(1)} %get-tuple-element.198, bf16[4,2048,128]{2,1,0:T(8,128)(2,1)S(1)} %get-tuple-element.210, s32[]{:T(128)} %get-tuple-element.195, ...), kind=kOutput, calls=%fused_computation.7.clone.1 | convolution fusion | flops 679608320 | bytes 12345349 | tf_op jit(solution)/shard_map/while/body/eval_jaxpr/htk,kd->htd/dot_general | solution.py:46
  256.3 2.7 bitcast_reduce_fusion.2
  259.0 4.0 %copy-done = f32[2048,160,8]{0,1,2:T(8,128)} copy-done((f32[2048,160,8]{0,1,2:T(8,128)}, f32[2048,160,8]{0,1,2:T(8,128)S(1)}, u32[]{:S(2)}) %copy-start) | copy-done | bytes 10485784 | tf_op jit(solution)/shard_map/while
  264.9 5.1 %fusion.85 = f32[8,160,128]{2,1,0:T(8,128)S(1)} fusion(f32[2048,160,8]{0,1,2:T(8,128)} %copy-done, f32[8,160]{1,0:T(8,128)S(1)} %get-tuple-element.181, f32[8,160,128]{2,1,0:T(8,128)S(1)} %get-tuple-element.198, bf16[4,2048,128]{2,1,0:T(8,128)(2,1)S(1)} %get-tuple-element.210, s32[]{:T(128)} %get-tuple-element.195, ...), kind=kOutput, calls=%fused_computation.7.clone.1 | convolution fusion | flops 679608320 | bytes 12345349 | tf_op jit(solution)/shard_map/while/body/eval_jaxpr/htk,kd->htd/dot_general | solution.py:46
  270.0 2.7 bitcast_reduce_fusion.2
  272.7 4.0 %copy-done = f32[2048,160,8]{0,1,2:T(8,128)} copy-done((f32[2048,160,8]{0,1,2:T(8,128)}, f32[2048,160,8]{0,1,2:T(8,128)S(1)}, u32[]{:S(2)}) %copy-start) | copy-done | bytes 10485784 | tf_op jit(solution)/shard_map/while
  278.6 5.1 %fusion.85 = f32[8,160,128]{2,1,0:T(8,128)S(1)} fusion(f32[2048,160,8]{0,1,2:T(8,128)} %copy-done, f32[8,160]{1,0:T(8,128)S(1)} %get-tuple-element.181, f32[8,160,128]{2,1,0:T(8,128)S(1)} %get-tuple-element.198, bf16[4,2048,128]{2,1,0:T(8,128)(2,1)S(1)} %get-tuple-element.210, s32[]{:T(128)} %get-tuple-element.195, ...), kind=kOutput, calls=%fused_computation.7.clone.1 | convolution fusion | flops 679608320 | bytes 12345349 | tf_op jit(solution)/shard_map/while/body/eval_jaxpr/htk,kd->htd/dot_general | solution.py:46
  283.8 2.7 bitcast_reduce_fusion.2
  286.5 4.0 %copy-done = f32[2048,160,8]{0,1,2:T(8,128)} copy-done((f32[2048,160,8]{0,1,2:T(8,128)}, f32[2048,160,8]{0,1,2:T(8,128)S(1)}, u32[]{:S(2)}) %copy-start) | copy-done | bytes 10485784 | tf_op jit(solution)/shard_map/while
  292.4 5.1 %fusion.85 = f32[8,160,128]{2,1,0:T(8,128)S(1)} fusion(f32[2048,160,8]{0,1,2:T(8,128)} %copy-done, f32[8,160]{1,0:T(8,128)S(1)} %get-tuple-element.181, f32[8,160,128]{2,1,0:T(8,128)S(1)} %get-tuple-element.198, bf16[4,2048,128]{2,1,0:T(8,128)(2,1)S(1)} %get-tuple-element.210, s32[]{:T(128)} %get-tuple-element.195, ...), kind=kOutput, calls=%fused_computation.7.clone.1 | convolution fusion | flops 679608320 | bytes 12345349 | tf_op jit(solution)/shard_map/while/body/eval_jaxpr/htk,kd->htd/dot_general | solution.py:46
  297.6 3.8 %collective-permute-start.10 = (f32[4,160,128]{2,1,0:T(8,128)S(1)}, f32[4,160,128]{2,1,0:T(8,128)S(1)}, u32[]{:S(2)}, u32[]{:S(2)}) collective-permute-start(f32[4,160,128]{2,1,0:T(8,128)S(1)} %get-tuple-element.107), channel_id=1, source_target_pairs={{16,18},{17,19},{18,16},{19,17},{20,22},{21,23},{22,20},{23,21},{2... | collective-permute-start | bytes 983048 | tf_op jit(solution)/shard_map/ppermute | solution.py:177
  301.5 5.9 %collective-permute-start.11 = (f32[4,160]{1,0:T(4,128)S(1)}, f32[4,160]{1,0:T(4,128)S(1)}, u32[]{:S(2)}, u32[]{:S(2)}) collective-permute-start(f32[4,160]{1,0:T(4,128)S(1)} %get-tuple-element.115), channel_id=1, source_target_pairs={{16,18},{17,19},{18,16},{19,17},{20,22},{21,23},{22,20},{23,21},{2... | collective-permute-start | bytes 7688 | tf_op jit(solution)/shard_map/ppermute | solution.py:177
  307.6 3.8 %collective-permute-start.15 = (f32[4,160]{1,0:T(4,128)S(1)}, f32[4,160]{1,0:T(4,128)S(1)}, u32[]{:S(2)}, u32[]{:S(2)}) collective-permute-start(f32[4,160]{1,0:T(4,128)S(1)} %get-tuple-element.117), channel_id=1, source_target_pairs={{16,18},{17,19},{18,16},{19,17},{20,22},{21,23},{22,20},{23,21},{2... | collective-permute-start | bytes 7688 | tf_op jit(solution)/shard_map/ppermute | solution.py:177
  311.4 5.8 %collective-permute-done.11 = f32[4,160]{1,0:T(4,128)S(1)} collective-permute-done((f32[4,160]{1,0:T(4,128)S(1)}, f32[4,160]{1,0:T(4,128)S(1)}, u32[]{:S(2)}, u32[]{:S(2)}) %collective-permute-start.11) | collective-permute-done | bytes 2592 | tf_op jit(solution)/shard_map/ppermute | solution.py:177
  318.3 2.4 collective-permute-done.16
  (98 shorter events, 41.2 us)
Async XLA Ops:
  6.5 68.8 %copy-start.8 = (bf16[512,128]{1,0:T(8,128)(2,1)S(1)}, bf16[512,128]{1,0:T(8,128)(2,1)}, u32[]{:S(2)}) copy-start(bf16[512,128]{1,0:T(8,128)(2,1)} %param.10) | copy-start | bytes 393220
  6.5 68.8 %copy-start.7 = (bf16[512,512]{1,0:T(8,128)(2,1)S(1)}, bf16[512,512]{1,0:T(8,128)(2,1)}, u32[]{:S(2)}) copy-start(bf16[512,512]{1,0:T(8,128)(2,1)} %param.9) | copy-start | bytes 1572868
  6.5 206.2 %reduce-scatter.4.cloned.1.call-start = ((), (), s32[]{:S(2)}) async-start(), calls=%async_computation.2 | async-start | bytes 6963200
  88.1 1.0 copy-start.1
  88.1 3.3 %copy-start.4 = (s32[16]{0:T(128)S(1)}, s32[16]{0:T(128)}, u32[]{:S(2)}) copy-start(s32[16]{0:T(128)} %param.13) | copy-start | bytes 196
  88.1 15.7 %copy-start.9 = (s32[16]{0:T(128)S(1)}, s32[16]{0:T(128)}, u32[]{:S(2)}) copy-start(s32[16]{0:T(128)} %param.12) | copy-start | bytes 196
  89.2 16.9 %collective-permute-start = (bf16[2,1024,128]{2,1,0:T(8,128)(2,1)S(1)}, bf16[2,1024,128]{2,1,0:T(8,128)(2,1)S(1)}, u32[]{:S(2)}, u32[]{:S(2)}) collective-permute-start(bf16[2,1024,128]{2,1,0:T(8,128)(2,1)S(1)} %copy-done.1), channel_id=1, source_target_pairs={{0,16},{16,0},{32,48},{48,32},{64,80},{80,64},{96,112},{112,96},{1... | collective-permute-start | bytes 1572872 | tf_op jit(solution)/shard_map/ppermute | solution.py:14
  104.5 8.5 %copy-start.6 = (f32[64]{0:T(128)}, f32[64]{0:T(128)S(1)}, u32[]{:S(2)}) copy-start(f32[64]{0:T(128)S(1)} %negate_power_fusion) | copy-start | bytes 772
  105.0 8.0 %copy-start.5 = (f32[160]{0:T(256)}, f32[160]{0:T(256)S(1)}, u32[]{:S(2)}) copy-start(f32[160]{0:T(256)S(1)} %add_convert_fusion.1) | copy-start | bytes 1924
  107.5 10.8 %collective-permute-start.1 = (bf16[1024,256]{1,0:T(8,128)(2,1)}, bf16[1024,256]{1,0:T(8,128)(2,1)}, u32[]{:S(2)}, u32[]{:S(2)}) collective-permute-start(bf16[1024,256]{1,0:T(8,128)(2,1)} %get-tuple-element.98), channel_id=1, source_target_pairs={{0,1},{1,0},{2,3},{3,2},{4,5},{5,4},{6,7},{7,6},{8,9},{9,8},{10,11... | collective-permute-start | bytes 1572872 | tf_op jit(solution)/shard_map/ppermute | solution.py:150
  107.5 15.1 %collective-permute-start.2 = (bf16[1024,256]{1,0:T(8,128)(2,1)}, bf16[1024,256]{1,0:T(8,128)(2,1)}, u32[]{:S(2)}, u32[]{:S(2)}) collective-permute-start(bf16[1024,256]{1,0:T(8,128)(2,1)} %get-tuple-element.99), channel_id=1, source_target_pairs={{0,4},{1,5},{2,6},{3,7},{4,0},{5,1},{6,2},{7,3},{8,12},{9,13},{10,... | collective-permute-start | bytes 1572872 | tf_op jit(solution)/shard_map/ppermute | solution.py:150
  109.8 27.3 %collective-permute-start.3 = (bf16[1024,256]{1,0:T(8,128)(2,1)}, bf16[1024,256]{1,0:T(8,128)(2,1)}, u32[]{:S(2)}, u32[]{:S(2)}) collective-permute-start(bf16[1024,256]{1,0:T(8,128)(2,1)} %get-tuple-element.100), channel_id=1, source_target_pairs={{0,5},{1,4},{2,7},{3,6},{4,1},{5,0},{6,3},{7,2},{8,13},{9,12},{10,... | collective-permute-start | bytes 1572872 | tf_op jit(solution)/shard_map/ppermute | solution.py:150
  114.9 38.1 %collective-permute-start.4 = (bf16[1024,256]{1,0:T(8,128)(2,1)S(1)}, bf16[1024,256]{1,0:T(8,128)(2,1)S(1)}, u32[]{:S(2)}, u32[]{:S(2)}) collective-permute-start(bf16[1024,256]{1,0:T(8,128)(2,1)S(1)} %get-tuple-element.101), channel_id=1, source_target_pairs={{0,8},{1,9},{2,10},{3,11},{4,12},{5,13},{6,14},{7,15},{8,0},{9,1},... | collective-permute-start | bytes 1572872 | tf_op jit(solution)/shard_map/ppermute | solution.py:150
  118.2 46.2 %collective-permute-start.5 = (bf16[1024,256]{1,0:T(8,128)(2,1)S(1)}, bf16[1024,256]{1,0:T(8,128)(2,1)S(1)}, u32[]{:S(2)}, u32[]{:S(2)}) collective-permute-start(bf16[1024,256]{1,0:T(8,128)(2,1)S(1)} %get-tuple-element.102), channel_id=1, source_target_pairs={{0,9},{1,8},{2,11},{3,10},{4,13},{5,12},{6,15},{7,14},{8,1},{9,0},... | collective-permute-start | bytes 1572872 | tf_op jit(solution)/shard_map/ppermute | solution.py:150
  118.4 46.0 %collective-permute-start.6 = (bf16[1024,256]{1,0:T(8,128)(2,1)S(1)}, bf16[1024,256]{1,0:T(8,128)(2,1)S(1)}, u32[]{:S(2)}, u32[]{:S(2)}) collective-permute-start(bf16[1024,256]{1,0:T(8,128)(2,1)S(1)} %fusion.43), channel_id=1, source_target_pairs={{0,12},{1,13},{2,14},{3,15},{4,8},{5,9},{6,10},{7,11},{8,4},{9,5},... | collective-permute-start | bytes 1572872 | tf_op jit(solution)/shard_map/ppermute | solution.py:150
  122.7 56.8 %collective-permute-start.7 = (bf16[1024,256]{1,0:T(8,128)(2,1)S(1)}, bf16[1024,256]{1,0:T(8,128)(2,1)S(1)}, u32[]{:S(2)}, u32[]{:S(2)}) collective-permute-start(bf16[1024,256]{1,0:T(8,128)(2,1)S(1)} %get-tuple-element.97), channel_id=1, source_target_pairs={{0,13},{1,12},{2,15},{3,14},{4,9},{5,8},{6,11},{7,10},{8,5},{9,4},... | collective-permute-start | bytes 1572872 | tf_op jit(solution)/shard_map/ppermute | solution.py:150
  221.3 21.3 %copy-start.2 = (bf16[160,128]{0,1:T(8,128)(2,1)}, bf16[160,128]{0,1:T(8,128)(2,1)S(1)}, u32[]{:S(2)}) copy-start(bf16[160,128]{0,1:T(8,128)(2,1)S(1)} %fusion.52) | copy-start | bytes 122884
  221.3 6.7 %collective-permute-start.13 = (bf16[160,1,128]{0,2,1:T(8,128)(2,1)S(1)}, bf16[160,1,128]{0,2,1:T(8,128)(2,1)S(1)}, u32[]{:S(2)}, u32[]{:S(2)}) collective-permute-start(bf16[160,1,128]{0,2,1:T(8,128)(2,1)S(1)} %bitcast.115), channel_id=1, source_target_pairs={{0,16},{16,0},{32,48},{48,32},{64,80},{80,64},{96,112},{112,96},{1... | collective-permute-start | bytes 122888 | tf_op jit(solution)/shard_map/ppermute | solution.py:14
  224.9 17.6 %collective-permute-start.8 = (bf16[160,4,128]{2,0,1:T(8,128)(2,1)S(1)}, bf16[160,4,128]{2,0,1:T(8,128)(2,1)S(1)}, u32[]{:S(2)}, u32[]{:S(2)}) collective-permute-start(bf16[160,4,128]{2,0,1:T(8,128)(2,1)S(1)} %pad_maximum_fusion.1), channel_id=1, source_target_pairs={{0,18},{1,19},{2,16},{3,17},{4,22},{5,23},{6,20},{7,21},{8,26},{9,... | collective-permute-start | bytes 491528 | tf_op jit(solution)/shard_map/ppermute | solution.py:160
  225.0 17.5 %collective-permute-start.9 = (bf16[160,4,128]{2,0,1:T(8,128)(2,1)S(1)}, bf16[160,4,128]{2,0,1:T(8,128)(2,1)S(1)}, u32[]{:S(2)}, u32[]{:S(2)}) collective-permute-start(bf16[160,4,128]{2,0,1:T(8,128)(2,1)S(1)} %pad_maximum_fusion.1), channel_id=1, source_target_pairs={{16,18},{17,19},{18,16},{19,17},{20,22},{21,23},{22,20},{23,21},{2... | collective-permute-start | bytes 491528 | tf_op jit(solution)/shard_map/ppermute | solution.py:161
  242.5 78.2 %copy-start.3 = (bf16[160,128]{0,1:T(8,128)(2,1)S(1)}, bf16[160,128]{0,1:T(8,128)(2,1)}, u32[]{:S(2)}) copy-start(bf16[160,128]{0,1:T(8,128)(2,1)} %copy-done.2) | copy-start | bytes 122884
  242.5 78.2 %copy-start.10 = (f32[160]{0:T(256)S(1)}, f32[160]{0:T(256)}, u32[]{:S(2)}) copy-start(f32[160]{0:T(256)} %fusion.66) | copy-start | bytes 1924
  245.2 4.0 %copy-start = (f32[2048,160,8]{0,1,2:T(8,128)}, f32[2048,160,8]{0,1,2:T(8,128)S(1)}, u32[]{:S(2)}) copy-start(f32[2048,160,8]{0,1,2:T(8,128)S(1)} %get-tuple-element.180) | copy-start | bytes 31457284 | tf_op jit(solution)/shard_map/while
  259.0 4.0 %copy-start = (f32[2048,160,8]{0,1,2:T(8,128)}, f32[2048,160,8]{0,1,2:T(8,128)S(1)}, u32[]{:S(2)}) copy-start(f32[2048,160,8]{0,1,2:T(8,128)S(1)} %get-tuple-element.180) | copy-start | bytes 31457284 | tf_op jit(solution)/shard_map/while
  272.7 4.0 %copy-start = (f32[2048,160,8]{0,1,2:T(8,128)}, f32[2048,160,8]{0,1,2:T(8,128)S(1)}, u32[]{:S(2)}) copy-start(f32[2048,160,8]{0,1,2:T(8,128)S(1)} %get-tuple-element.180) | copy-start | bytes 31457284 | tf_op jit(solution)/shard_map/while
  286.5 4.0 %copy-start = (f32[2048,160,8]{0,1,2:T(8,128)}, f32[2048,160,8]{0,1,2:T(8,128)S(1)}, u32[]{:S(2)}) copy-start(f32[2048,160,8]{0,1,2:T(8,128)S(1)} %get-tuple-element.180) | copy-start | bytes 31457284 | tf_op jit(solution)/shard_map/while
  297.6 23.2 %collective-permute-start.10 = (f32[4,160,128]{2,1,0:T(8,128)S(1)}, f32[4,160,128]{2,1,0:T(8,128)S(1)}, u32[]{:S(2)}, u32[]{:S(2)}) collective-permute-start(f32[4,160,128]{2,1,0:T(8,128)S(1)} %get-tuple-element.107), channel_id=1, source_target_pairs={{16,18},{17,19},{18,16},{19,17},{20,22},{21,23},{22,20},{23,21},{2... | collective-permute-start | bytes 983048 | tf_op jit(solution)/shard_map/ppermute | solution.py:177
  301.4 19.4 %collective-permute-start.14 = (f32[4,160,128]{2,1,0:T(8,128)S(1)}, f32[4,160,128]{2,1,0:T(8,128)S(1)}, u32[]{:S(2)}, u32[]{:S(2)}) collective-permute-start(f32[4,160,128]{2,1,0:T(8,128)S(1)} %get-tuple-element.108), channel_id=1, source_target_pairs={{0,16},{1,17},{2,18},{3,19},{4,20},{5,21},{6,22},{7,23},{8,24},{9,... | collective-permute-start | bytes 983048 | tf_op jit(solution)/shard_map/ppermute | solution.py:176
  301.5 15.6 %collective-permute-start.11 = (f32[4,160]{1,0:T(4,128)S(1)}, f32[4,160]{1,0:T(4,128)S(1)}, u32[]{:S(2)}, u32[]{:S(2)}) collective-permute-start(f32[4,160]{1,0:T(4,128)S(1)} %get-tuple-element.115), channel_id=1, source_target_pairs={{16,18},{17,19},{18,16},{19,17},{20,22},{21,23},{22,20},{23,21},{2... | collective-permute-start | bytes 7688 | tf_op jit(solution)/shard_map/ppermute | solution.py:177
  307.5 10.9 %collective-permute-start.12 = (f32[4,160]{1,0:T(4,128)S(1)}, f32[4,160]{1,0:T(4,128)S(1)}, u32[]{:S(2)}, u32[]{:S(2)}) collective-permute-start(f32[4,160]{1,0:T(4,128)S(1)} %get-tuple-element.116), channel_id=1, source_target_pairs={{0,16},{1,17},{2,18},{3,19},{4,20},{5,21},{6,22},{7,23},{8,24},{9,... | collective-permute-start | bytes 7688 | tf_op jit(solution)/shard_map/ppermute | solution.py:176
  307.6 10.8 %collective-permute-start.15 = (f32[4,160]{1,0:T(4,128)S(1)}, f32[4,160]{1,0:T(4,128)S(1)}, u32[]{:S(2)}, u32[]{:S(2)}) collective-permute-start(f32[4,160]{1,0:T(4,128)S(1)} %get-tuple-element.117), channel_id=1, source_target_pairs={{16,18},{17,19},{18,16},{19,17},{20,22},{21,23},{22,20},{23,21},{2... | collective-permute-start | bytes 7688 | tf_op jit(solution)/shard_map/ppermute | solution.py:177
  317.1 3.6 %collective-permute-start.16 = (f32[4,160]{1,0:T(4,128)S(1)}, f32[4,160]{1,0:T(4,128)S(1)}, u32[]{:S(2)}, u32[]{:S(2)}) collective-permute-start(f32[4,160]{1,0:T(4,128)S(1)} %get-tuple-element.118), channel_id=1, source_target_pairs={{0,16},{1,17},{2,18},{3,19},{4,20},{5,21},{6,22},{7,23},{8,24},{9,... | collective-permute-start | bytes 7688 | tf_op jit(solution)/shard_map/ppermute | solution.py:176
Sparse Core Ops, SparseCore 0:
  88.3 124.3 reduce-scatter.3
